TPU v7x, 512 devices: a whole 4x8x8 slice. The times are simulated.
512 devices in a mesh: gx: 32 (over z, y_hi, core), gy: 16 (over x, y_lo).
Axes of the slice: x: 4, y: 8 (y_hi: 2, y_lo: 4; y = y_hi * 4 + y_lo), z: 8, core: 2. Of those that a mesh axis runs over, the one named last changes fastest.
Arguments:
- design: float32 [256, 128, 128], P('gx', 'gy'), may hold values from 0.06 to 0.9
- passive: int32 [256, 128, 128], P('gx', 'gy'), may hold values 0 or 1
- basis_pairs: float32 [4, 2, 3, 256, 128, 128], P(None, None, None, 'gx', 'gy'), may hold values from -6 to 6
- supports: int32 [256, 128, 128], P('gx', 'gy'), may hold values 0 or 1
- stiffness: float32 [24, 24], replicated, may hold values from -1.25 to 1.25
- mass_matrix: float32 [24, 24], replicated, may hold values from -1.25 to 1.25
- volume_fraction: float32 [64], replicated, may hold values from 0.26 to 0.36
Outputs:
- sensitivity: float32 [256, 128, 128], P('gx', 'gy')
- design_next: float32 [256, 128, 128], P('gx', 'gy')
All inputs are finite; a program needn't handle non-finite values. No bound on the sum of `passive` or of `supports` on one device may be relied on, other than what follows from the above.
Results may differ from a plain program's by a relative error of at most 0.0003.
Values sent between devices are 32-bit elements; how exact they have to be, the bound alone decides.
No kernel may reach another device: no remote copies, remote signals or barrier semaphores. Data moves between devices by JAX's collectives and lax.ppermute only.
A program may use at most 64 MiB of HBM per device.

v0:
```python
import math
import jax
import jax.numpy as jnp
from jax import lax
from jax.sharding import PartitionSpec as P

BISECT = 6
REGIONS = 64
PENALTY_SCALE = 3.0 * (1.0 - 0.001)
OMEGA_SQUARED = 0.5
MOVE_LIMIT = 0.2


def with_halo(cells, sides, width):
    for axis, dim in sides:
        count = lax.axis_size(axis)
        ends = count - 1
        head = lax.slice_in_dim(cells, 0, width, axis=dim)
        tail = lax.slice_in_dim(cells, cells.shape[dim] - width, cells.shape[dim], axis=dim)
        cells = jnp.concatenate(
            [
                lax.ppermute(tail, axis, [(i, (i + 1) % count) for i in range(ends)]),
                cells,
                lax.ppermute(head, axis, [((i + 1) % count, i) for i in range(ends)]),
            ],
            axis=dim,
        )
    return cells


def from_behind(value, axis, steps):
    count = lax.axis_size(axis)
    initial, last = (max(0, -steps), min(count, count - steps))
    return lax.ppermute(value, axis, [(source, source + steps) for source in range(initial, last)])


def filter_taps():
    tap_list = []
    for offset_x in range(-2, 3):
        for offset_y in range(-2, 3):
            for offset_z in range(-2, 3):
                weight = 3.0 - math.sqrt(
                    offset_x * offset_x + offset_y * offset_y + offset_z * offset_z
                )
                if weight > 0.0:
                    tap_list.append((offset_x, offset_y, offset_z, weight))
    return tap_list


def stencil(padded, block_shape):
    result = jnp.zeros(block_shape, jnp.float32)
    for offset_x, offset_y, offset_z, weight in filter_taps():
        result = (
            result
            + weight
            * padded[
                2 + offset_x : 2 + offset_x + block_shape[0],
                2 + offset_y : 2 + offset_y + block_shape[1],
                2 + offset_z : 2 + offset_z + block_shape[2],
            ]
        )
    return result


def element_terms(extended, stiffness, mass_matrix):
    pair_count = extended.shape[0]
    cells_x = extended.shape[3] - 1
    cells_y = extended.shape[4] - 1
    cells_z = extended.shape[5] - 1
    stiff_energy = jnp.zeros((cells_x * cells_y * cells_z,), jnp.float32)
    mass_energy = jnp.zeros((cells_x * cells_y * cells_z,), jnp.float32)
    for pair_index in range(pair_count):
        vectors = []
        for member in range(2):
            row_list = []
            for corner_x in (0, 1):
                for corner_y in (0, 1):
                    for corner_z in (0, 1):
                        for component in range(3):
                            row_list.append(
                                extended[
                                    pair_index,
                                    member,
                                    component,
                                    corner_x : corner_x + cells_x,
                                    corner_y : corner_y + cells_y,
                                    corner_z : corner_z + cells_z,
                                ].reshape(-1)
                            )
            vectors.append(jnp.stack(row_list))
        state_rows, adjoint_rows = vectors
        stiff_energy = stiff_energy + jnp.sum(
            state_rows * jnp.dot(stiffness, adjoint_rows, precision=lax.Precision.HIGHEST), axis=0
        )
        mass_energy = mass_energy + jnp.sum(
            state_rows * jnp.dot(mass_matrix, adjoint_rows, precision=lax.Precision.HIGHEST), axis=0
        )
    return (
        stiff_energy.reshape(cells_x, cells_y, cells_z),
        mass_energy.reshape(cells_x, cells_y, cells_z),
    )


def shards(design, passive, basis_pairs, supports, stiffness, mass_matrix, volume_fraction):
    block_shape = design.shape
    size_x, size_y, size_z = block_shape
    devices_x = lax.axis_size("gx")
    devices_y = lax.axis_size("gy")
    index_x = lax.axis_index("gx")
    index_y = lax.axis_index("gy")
    grid_x = size_x * devices_x
    grid_y = size_y * devices_y
    spread_x = jnp.arange(size_x + 4, dtype=jnp.int32) + index_x * size_x - 2
    spread_y = jnp.arange(size_y + 4, dtype=jnp.int32) + index_y * size_y - 2
    valid_x = ((spread_x >= 0) & (spread_x < grid_x)).astype(jnp.float32)
    valid_y = ((spread_y >= 0) & (spread_y < grid_y)).astype(jnp.float32)
    valid_z = jnp.pad(jnp.ones((size_z,), jnp.float32), 2)
    inside = valid_x[:, None, None] * valid_y[None, :, None] * valid_z[None, None, :]
    weight_sum = stencil(inside, block_shape)
    design_wide = with_halo(design, (("gx", 0), ("gy", 1)), 2)
    design_wide = jnp.pad(design_wide, ((0, 0), (0, 0), (2, 2)))
    physical = jnp.where(passive == 1, 1.0, stencil(design_wide, block_shape) / weight_sum)
    fields = basis_pairs * (1 - supports).astype(jnp.float32)
    rim_first = from_behind(fields[:, :, :, :1], "gx", -1)
    widened = jnp.concatenate([fields, rim_first], axis=3)
    rim_second = from_behind(widened[:, :, :, :, :1], "gy", -1)
    extended = jnp.concatenate([widened, rim_second], axis=4)
    extended = jnp.pad(extended, ((0, 0), (0, 0), (0, 0), (0, 0), (0, 0), (0, 1)))
    stiff_energy, mass_energy = element_terms(extended, stiffness, mass_matrix)
    raw_sensitivity = -(
        PENALTY_SCALE * physical * physical * stiff_energy - OMEGA_SQUARED * mass_energy
    )
    raw_sensitivity = jnp.where(passive == 1, 0.0, raw_sensitivity)
    scaled_wide = with_halo(raw_sensitivity / weight_sum, (("gx", 0), ("gy", 1)), 2)
    scaled_wide = jnp.pad(scaled_wide, ((0, 0), (0, 0), (2, 2)))
    sensitivity = stencil(scaled_wide, block_shape)
    benefit = jnp.maximum(-sensitivity, 0.0)
    floor_value = jnp.maximum(design - MOVE_LIMIT, 0.0)
    ceiling = jnp.minimum(design + MOVE_LIMIT, 1.0)
    band_cells = size_z // REGIONS
    target = volume_fraction * float(grid_x * grid_y * band_cells)

    def candidate(multiplier):
        per_cell = jnp.repeat(multiplier, band_cells)[None, None, :]
        trial = design * jnp.sqrt(benefit / per_cell)
        return jnp.where(passive == 1, 1.0, jnp.minimum(ceiling, jnp.maximum(floor_value, trial)))

    def region_sum(field):
        return jnp.sum(field, axis=(0, 1)).reshape(REGIONS, band_cells).sum(axis=1)

    levels = BISECT

    def bisect_round(round_index, bracket):
        low_end, high_end = bracket
        level_nodes = [(low_end, high_end)]
        midpoints = []
        for depth in range(levels):
            next_nodes = []
            for node_low, node_high in level_nodes:
                middle = jnp.sqrt(node_low * node_high)
                midpoints.append(middle)
                next_nodes.append((node_low, middle))
                next_nodes.append((middle, node_high))
            level_nodes = next_nodes
        trial_multipliers = jnp.stack(midpoints)
        per_cell = jnp.repeat(trial_multipliers, band_cells, axis=1)[:, None, None, :]
        trial = design[None] * jnp.sqrt(benefit[None] / per_cell)
        fields_of = jnp.where(
            passive[None] == 1,
            1.0,
            jnp.minimum(ceiling[None], jnp.maximum(floor_value[None], trial)),
        )
        partial_volumes = (
            jnp.sum(fields_of, axis=(1, 2)).reshape(len(midpoints), REGIONS, band_cells).sum(axis=2)
        )
        volumes = lax.psum(partial_volumes, ("gx", "gy"))
        position = jnp.zeros((REGIONS,), jnp.int32)
        for depth in range(levels):
            middle = jnp.sqrt(low_end * high_end)
            heap_index = position + (2**depth - 1)
            chosen = jnp.take_along_axis(volumes, heap_index[None, :], axis=0)[0]
            heavier = chosen > target
            low_end = jnp.where(heavier, middle, low_end)
            high_end = jnp.where(heavier, high_end, middle)
            position = 2 * position + heavier.astype(jnp.int32)
        return (low_end, high_end)

    start = (jnp.full((REGIONS,), 0.0001, jnp.float32), jnp.full((REGIONS,), 10000.0, jnp.float32))
    low_end, high_end = bisect_round(0, start)
    design_next = candidate(jnp.sqrt(low_end * high_end))
    return (sensitivity, design_next)


def solution(mesh):
    placed = (
        P("gx", "gy", None),
        P("gx", "gy", None),
        P(None, None, None, "gx", "gy", None),
        P("gx", "gy", None),
        P(),
        P(),
        P(),
    )
    return jax.shard_map(
        shards,
        mesh=mesh,
        in_specs=placed,
        out_specs=(P("gx", "gy", None), P("gx", "gy", None)),
        check_vma=False,
    )
```

profile of v0, /device:TPU:1, one launch (start us, length us, event | category | flops | bytes accessed | tf_op | source)
XLA Modules:
  0.0 233.9 jit_solution(4660837941216454200)
XLA Ops:
  1.4 8.8 %collective-permute-start.1 = (f32[2,8,128]{2,1,0:T(8,128)S(1)}, f32[2,8,128]{2,1,0:T(8,128)S(1)}, u32[]{:S(2)}, u32[]{:S(2)}) collective-permute-start(f32[2,8,128]{2,1,0:T(8,128)S(1)} %get-tuple-element.214), channel_id=1, source_target_pairs={{16,0},{32,16},{48,32},{64,48},{80,64},{96,80},{112,96},{128,112},... | collective-permute-start | bytes 24584 | tf_op jit(solution)/shard_map/ppermute | solution.py:24
  10.2 2.0 collective-permute-start
  13.0 1.2 broadcast_multiply_fusion
  14.2 2.3 %collective-permute-start.4 = (f32[4,2,3,1,8,128]{5,4,3,2,1,0:T(8,128)S(1)}, f32[4,2,3,1,8,128]{5,4,3,2,1,0:T(8,128)S(1)}, u32[]{:S(2)}, u32[]{:S(2)}) collective-permute-start(f32[4,2,3,1,8,128]{5,4,3,2,1,0:T(8,128)S(1)} %slice.2424), channel_id=1, source_target_pairs={{16,0},{32,16},{48,32},{64,48},{80,64},{96,80},{112,96},{128,112},... | collective-permute-start | bytes 294920 | tf_op jit(solution)/shard_map/ppermute | solution.py:34
  18.3 2.3 collective-permute-start.2
  20.6 1.3 collective-permute-start.3
  22.4 2.7 %collective-permute-done.3 = f32[12,2,128]{2,1,0:T(2,128)S(1)} collective-permute-done((f32[12,2,128]{2,1,0:T(2,128)S(1)}, f32[12,2,128]{2,1,0:T(2,128)S(1)}, u32[]{:S(2)}, u32[]{:S(2)}) %collective-permute-start.3) | collective-permute-done | bytes 12320 | tf_op jit(solution)/shard_map/ppermute | solution.py:24
  25.4 1.3 collective-permute-start.5
  29.0 4.9 %collective-permute-done.5 = f32[4,2,3,9,1,128]{5,3,4,2,1,0:T(8,128)S(1)} collective-permute-done((f32[4,2,3,9,1,128]{5,3,4,2,1,0:T(8,128)S(1)}, f32[4,2,3,9,1,128]{5,3,4,2,1,0:T(8,128)S(1)}, u32[]{:S(2)}, u32[]{:S(2)}) %collective-permute-start.5) | collective-permute-done | bytes 110624 | tf_op jit(solution)/shard_map/ppermute | solution.py:34
  34.2 0.8 fusion.376
  35.1 1.0 pad_slice_fusion.79
  36.1 1.1 pad_slice_fusion.48
  37.1 0.9 fusion.372
  38.0 1.1 fusion.373
  39.1 0.9 fusion.374
  40.0 3.7 %stack.24 = f32[24,8192]{1,0:T(8,128)S(1)} concatenate(f32[1,8192]{1,0:T(1,128)} %bitcast.576, f32[1,8192]{1,0:T(1,128)} %bitcast.575, f32[1,8192]{1,0:T(1,128)} %bitcast.574, f32[1,8192]{1,0:T(1,128)} %bitcast.624, f32[1,8192]{1,0:T(1,128)} %bitcast.497, f32[1,8192]{1,0:T(1,128)} %bitcast.498, f32[1,8192]{1,0:T(1,128)} %bitcast.623, f32[1,8192]{1,0:T(1,128)} %bitcast.622, ...), dimensions={0} | concatenate | bytes 1572864 | tf_op jit(solution)/shard_map/stack | solution.py:90
  43.8 5.8 %stack.25 = f32[24,8192]{1,0:T(8,128)} concatenate(f32[1,8192]{1,0:T(1,128)} %bitcast.571, f32[1,8192]{1,0:T(1,128)} %bitcast.570, f32[1,8192]{1,0:T(1,128)} %bitcast.588, f32[1,8192]{1,0:T(1,128)} %bitcast.468, f32[1,8192]{1,0:T(1,128)} %bitcast.469, f32[1,8192]{1,0:T(1,128)} %bitcast.470, f32[1,8192]{1,0:T(1,128)} %bitcast.617, f32[1,8192]{1,0:T(1,128)} %bitcast.616, ...), dimensions={0} | concatenate | bytes 1572864 | tf_op jit(solution)/shard_map/stack | solution.py:90
  49.6 2.7 %fusion.17 = f32[8192]{0:T(1024)} fusion(f32[24,8192]{1,0:T(8,128)S(1)} %stack.24, f32[24,8192]{1,0:T(8,128)} %stack.25, f32[24,24]{1,0:T(8,128)S(1)} %copy-done), kind=kOutput, calls=%fused_computation.153 | convolution fusion | flops 57008128 | bytes 1607936 | tf_op jit(solution)/shard_map/dot_general | solution.py:96
  52.3 1.5 fusion.13
  53.8 3.7 %stack.31 = f32[24,8192]{1,0:T(8,128)S(1)} concatenate(f32[1,8192]{1,0:T(1,128)} %bitcast.564, f32[1,8192]{1,0:T(1,128)} %bitcast.584, f32[1,8192]{1,0:T(1,128)} %bitcast.580, f32[1,8192]{1,0:T(1,128)} %bitcast.514, f32[1,8192]{1,0:T(1,128)} %bitcast.515, f32[1,8192]{1,0:T(1,128)} %bitcast.516, f32[1,8192]{1,0:T(1,128)} %bitcast.531, f32[1,8192]{1,0:T(1,128)} %bitcast.530, ...), dimensions={0} | concatenate | bytes 1572864 | tf_op jit(solution)/shard_map/stack | solution.py:90
  57.5 5.8 %stack.30 = f32[24,8192]{1,0:T(8,128)} concatenate(f32[1,8192]{1,0:T(1,128)} %bitcast.558, f32[1,8192]{1,0:T(1,128)} %bitcast.557, f32[1,8192]{1,0:T(1,128)} %bitcast.556, f32[1,8192]{1,0:T(1,128)} %bitcast.466, f32[1,8192]{1,0:T(1,128)} %bitcast.479, f32[1,8192]{1,0:T(1,128)} %bitcast.480, f32[1,8192]{1,0:T(1,128)} %bitcast.513, f32[1,8192]{1,0:T(1,128)} %bitcast.512, ...), dimensions={0} | concatenate | bytes 1572864 | tf_op jit(solution)/shard_map/stack | solution.py:90
  63.3 2.7 %fusion.20 = f32[8192]{0:T(1024)} fusion(f32[24,8192]{1,0:T(8,128)} %stack.30, f32[24,8192]{1,0:T(8,128)S(1)} %stack.31, f32[24,24]{1,0:T(8,128)S(1)} %copy-done), kind=kOutput, calls=%fused_computation.156 | convolution fusion | flops 57008128 | bytes 1607936 | tf_op jit(solution)/shard_map/dot_general | solution.py:96
  66.0 1.5 fusion.16
  67.5 0.9 fusion.375
  68.4 1.0 pad_slice_fusion.49
  69.5 3.7 %stack.27 = f32[24,8192]{1,0:T(8,128)S(1)} concatenate(f32[1,8192]{1,0:T(1,128)} %bitcast.569, f32[1,8192]{1,0:T(1,128)} %bitcast.568, f32[1,8192]{1,0:T(1,128)} %bitcast.567, f32[1,8192]{1,0:T(1,128)} %bitcast.534, f32[1,8192]{1,0:T(1,128)} %bitcast.535, f32[1,8192]{1,0:T(1,128)} %bitcast.536, f32[1,8192]{1,0:T(1,128)} %bitcast.610, f32[1,8192]{1,0:T(1,128)} %bitcast.609, ...), dimensions={0} | concatenate | bytes 1572864 | tf_op jit(solution)/shard_map/stack | solution.py:90
  73.3 3.6 %stack.26 = f32[24,8192]{1,0:T(8,128)S(1)} concatenate(f32[1,8192]{1,0:T(1,128)S(1)} %bitcast.563, f32[1,8192]{1,0:T(1,128)S(1)} %bitcast.562, f32[1,8192]{1,0:T(1,128)S(1)} %bitcast.561, f32[1,8192]{1,0:T(1,128)S(1)} %bitcast.450, f32[1,8192]{1,0:T(1,128)S(1)} %bitcast.451, f32[1,8192]{1,0:T(1,128)S(1)} %bitcast.452, f32[1,8192]{1,0:T(1,128)} %bitcast.611, f32[1,8192]{1,0:T(1,128)} %bitcast.607, ...), dimensions={0} | concatenate | bytes 1572864 | tf_op jit(solution)/shard_map/stack | solution.py:90
  77.0 0.9 fusion.18
  78.0 0.9 fusion.14
  79.0 3.4 %stack.29 = f32[24,8192]{1,0:T(8,128)S(1)} concatenate(f32[1,8192]{1,0:T(1,128)S(1)} %bitcast.549, f32[1,8192]{1,0:T(1,128)S(1)} %bitcast.548, f32[1,8192]{1,0:T(1,128)S(1)} %bitcast.547, f32[1,8192]{1,0:T(1,128)S(1)} %bitcast.438, f32[1,8192]{1,0:T(1,128)S(1)} %bitcast.439, f32[1,8192]{1,0:T(1,128)S(1)} %bitcast.440, f32[1,8192]{1,0:T(1,128)} %bitcast.602, f32[1,8192]{1,0:T(1,128)} %bitcast.601, ...), dimensions={0} | concatenate | bytes 1572864 | tf_op jit(solution)/shard_map/stack | solution.py:90
  82.5 1.2 stack.28
  83.7 0.9 fusion.19
  84.6 0.9 fusion.15
  85.5 1.2 fusion.98
  86.8 8.2 %collective-permute-start.6 = (f32[2,8,128]{2,1,0:T(8,128)S(1)}, f32[2,8,128]{2,1,0:T(8,128)S(1)}, u32[]{:S(2)}, u32[]{:S(2)}) collective-permute-start(f32[2,8,128]{2,1,0:T(8,128)S(1)} %get-tuple-element.212), channel_id=1, source_target_pairs={{0,16},{16,32},{32,48},{48,64},{64,80},{80,96},{96,112},{112,128},... | collective-permute-start | bytes 24584 | tf_op jit(solution)/shard_map/ppermute | solution.py:22
  94.9 1.9 collective-permute-start.7
  96.9 6.9 %collective-permute-done.7 = f32[2,8,128]{2,1,0:T(8,128)S(1)} collective-permute-done((f32[2,8,128]{2,1,0:T(8,128)S(1)}, f32[2,8,128]{2,1,0:T(8,128)S(1)}, u32[]{:S(2)}, u32[]{:S(2)}) %collective-permute-start.7) | collective-permute-done | bytes 8224 | tf_op jit(solution)/shard_map/ppermute | solution.py:24
  103.8 3.1 %collective-permute-start.8 = (f32[12,2,128]{2,1,0:T(2,128)S(1)}, f32[12,2,128]{2,1,0:T(2,128)S(1)}, u32[]{:S(2)}, u32[]{:S(2)}) collective-permute-start(f32[12,2,128]{2,1,0:T(2,128)S(1)} %get-tuple-element.203), channel_id=1, source_target_pairs={{0,1},{1,2},{2,3},{3,4},{4,5},{5,6},{6,7},{7,8},{8,9},{9,10},{10,1... | collective-permute-start | bytes 36872 | tf_op jit(solution)/shard_map/ppermute | solution.py:22
  106.9 1.3 collective-permute-start.9
  108.4 5.7 %collective-permute-done.9 = f32[12,2,128]{2,1,0:T(2,128)S(1)} collective-permute-done((f32[12,2,128]{2,1,0:T(2,128)S(1)}, f32[12,2,128]{2,1,0:T(2,128)S(1)}, u32[]{:S(2)}, u32[]{:S(2)}) %collective-permute-start.9) | collective-permute-done | bytes 12320 | tf_op jit(solution)/shard_map/ppermute | solution.py:24
  114.9 0.9 fusion.12
  116.1 111.8 %psum.7 = f32[63,64]{1,0:T(8,128)S(1)} all-reduce(f32[63,64]{1,0:T(8,128)S(1)} %copy.118), channel_id=1, replica_groups=mesh['gx'=32,'gy'=16] {'gx','gy'}, use_global_device_ids=true, to_apply=%region_10.11 | all-reduce | flops 4032 | bytes 32256 | tf_op jit(solution)/shard_map/psum | solution.py:176
  227.9 0.8 gather_fusion
  228.8 0.8 gather_fusion.1
  229.6 0.8 gather_fusion.2
  230.5 0.8 gather_fusion.3
  231.3 0.8 gather_fusion.4
  232.2 0.8 gather_fusion.5
  (182 shorter events, 9.0 us)
Async XLA Ops:
  0.6 49.0 %copy-start = (f32[24,24]{1,0:T(8,128)S(1)}, f32[24,24]{1,0:T(8,128)}, u32[]{:S(2)}) copy-start(f32[24,24]{1,0:T(8,128)} %param.14) | copy-start | bytes 6916
  0.6 17.0 %copy-start.3 = (f32[8,8,128]{2,1,0:T(8,128)S(1)}, f32[8,8,128]{2,1,0:T(8,128)}, u32[]{:S(2)}) copy-start(f32[8,8,128]{2,1,0:T(8,128)} %param.9) | copy-start | bytes 98308
  1.4 16.8 %collective-permute-start.1 = (f32[2,8,128]{2,1,0:T(8,128)S(1)}, f32[2,8,128]{2,1,0:T(8,128)S(1)}, u32[]{:S(2)}, u32[]{:S(2)}) collective-permute-start(f32[2,8,128]{2,1,0:T(8,128)S(1)} %get-tuple-element.214), channel_id=1, source_target_pairs={{16,0},{32,16},{48,32},{64,48},{80,64},{96,80},{112,96},{128,112},... | collective-permute-start | bytes 24584 | tf_op jit(solution)/shard_map/ppermute | solution.py:24
  10.2 7.4 %collective-permute-start = (f32[2,8,128]{2,1,0:T(8,128)S(1)}, f32[2,8,128]{2,1,0:T(8,128)S(1)}, u32[]{:S(2)}, u32[]{:S(2)}) collective-permute-start(f32[2,8,128]{2,1,0:T(8,128)S(1)} %get-tuple-element.215), channel_id=1, source_target_pairs={{0,16},{16,32},{32,48},{48,64},{64,80},{80,96},{96,112},{112,128},... | collective-permute-start | bytes 24584 | tf_op jit(solution)/shard_map/ppermute | solution.py:22
  14.2 11.1 %collective-permute-start.4 = (f32[4,2,3,1,8,128]{5,4,3,2,1,0:T(8,128)S(1)}, f32[4,2,3,1,8,128]{5,4,3,2,1,0:T(8,128)S(1)}, u32[]{:S(2)}, u32[]{:S(2)}) collective-permute-start(f32[4,2,3,1,8,128]{5,4,3,2,1,0:T(8,128)S(1)} %slice.2424), channel_id=1, source_target_pairs={{16,0},{32,16},{48,32},{64,48},{80,64},{96,80},{112,96},{128,112},... | collective-permute-start | bytes 294920 | tf_op jit(solution)/shard_map/ppermute | solution.py:34
  18.3 4.1 %collective-permute-start.2 = (f32[12,2,128]{2,1,0:T(2,128)S(1)}, f32[12,2,128]{2,1,0:T(2,128)S(1)}, u32[]{:S(2)}, u32[]{:S(2)}) collective-permute-start(f32[12,2,128]{2,1,0:T(2,128)S(1)} %get-tuple-element.205), channel_id=1, source_target_pairs={{0,1},{1,2},{2,3},{3,4},{4,5},{5,6},{6,7},{7,8},{8,9},{9,10},{10,1... | collective-permute-start | bytes 36872 | tf_op jit(solution)/shard_map/ppermute | solution.py:22
  20.6 4.6 %collective-permute-start.3 = (f32[12,2,128]{2,1,0:T(2,128)S(1)}, f32[12,2,128]{2,1,0:T(2,128)S(1)}, u32[]{:S(2)}, u32[]{:S(2)}) collective-permute-start(f32[12,2,128]{2,1,0:T(2,128)S(1)} %get-tuple-element.206), channel_id=1, source_target_pairs={{1,0},{2,1},{3,2},{4,3},{5,4},{6,5},{7,6},{8,7},{9,8},{10,9},{11,1... | collective-permute-start | bytes 36872 | tf_op jit(solution)/shard_map/ppermute | solution.py:24
  25.4 8.5 %collective-permute-start.5 = (f32[4,2,3,9,1,128]{5,3,4,2,1,0:T(8,128)S(1)}, f32[4,2,3,9,1,128]{5,3,4,2,1,0:T(8,128)S(1)}, u32[]{:S(2)}, u32[]{:S(2)}) collective-permute-start(f32[4,2,3,9,1,128]{5,3,4,2,1,0:T(8,128)S(1)} %copy.114), channel_id=1, source_target_pairs={{1,0},{2,1},{3,2},{4,3},{5,4},{6,5},{7,6},{8,7},{9,8},{10,9},{11,1... | collective-permute-start | bytes 331784 | tf_op jit(solution)/shard_map/ppermute | solution.py:34
  43.8 8.5 %copy-start.4 = (f32[24,24]{1,0:T(8,128)S(1)}, f32[24,24]{1,0:T(8,128)}, u32[]{:S(2)}) copy-start(f32[24,24]{1,0:T(8,128)} %param.13) | copy-start | bytes 6916
  68.3 4.8 %copy-start.10 = (f32[1,1,1,8,8,128]{5,4,3,2,1,0:T(8,128)S(1)}, f32[1,1,1,8,8,128]{5,4,3,2,1,0:T(8,128)}, u32[]{:S(2)}) copy-start(f32[1,1,1,8,8,128]{5,4,3,2,1,0:T(8,128)} %get-tuple-element.17) | copy-start | bytes 98308
  68.3 4.8 %copy-start.11 = (f32[1,1,1,8,8,128]{5,4,3,2,1,0:T(8,128)S(1)}, f32[1,1,1,8,8,128]{5,4,3,2,1,0:T(8,128)}, u32[]{:S(2)}) copy-start(f32[1,1,1,8,8,128]{5,4,3,2,1,0:T(8,128)} %get-tuple-element.18) | copy-start | bytes 98308
  68.3 4.8 %copy-start.12 = (f32[1,1,1,8,8,128]{5,4,3,2,1,0:T(8,128)S(1)}, f32[1,1,1,8,8,128]{5,4,3,2,1,0:T(8,128)}, u32[]{:S(2)}) copy-start(f32[1,1,1,8,8,128]{5,4,3,2,1,0:T(8,128)} %get-tuple-element.19) | copy-start | bytes 98308
  68.3 4.8 %copy-start.13 = (f32[1,1,1,8,8,128]{5,4,3,2,1,0:T(8,128)S(1)}, f32[1,1,1,8,8,128]{5,4,3,2,1,0:T(8,128)}, u32[]{:S(2)}) copy-start(f32[1,1,1,8,8,128]{5,4,3,2,1,0:T(8,128)} %get-tuple-element.20) | copy-start | bytes 98308
  68.4 4.8 %copy-start.14 = (f32[1,1,1,8,8,128]{5,4,3,2,1,0:T(8,128)S(1)}, f32[1,1,1,8,8,128]{5,4,3,2,1,0:T(8,128)}, u32[]{:S(2)}) copy-start(f32[1,1,1,8,8,128]{5,4,3,2,1,0:T(8,128)} %get-tuple-element.21) | copy-start | bytes 98308
  68.4 4.8 %copy-start.15 = (f32[1,1,1,8,8,128]{5,4,3,2,1,0:T(8,128)S(1)}, f32[1,1,1,8,8,128]{5,4,3,2,1,0:T(8,128)}, u32[]{:S(2)}) copy-start(f32[1,1,1,8,8,128]{5,4,3,2,1,0:T(8,128)} %get-tuple-element.22) | copy-start | bytes 98308
  68.4 4.8 %copy-start.16 = (f32[1,1,1,8,8,128]{5,4,3,2,1,0:T(8,128)S(1)}, f32[1,1,1,8,8,128]{5,4,3,2,1,0:T(8,128)}, u32[]{:S(2)}) copy-start(f32[1,1,1,8,8,128]{5,4,3,2,1,0:T(8,128)} %get-tuple-element.23) | copy-start | bytes 98308
  68.4 4.8 %copy-start.17 = (f32[1,1,1,8,8,128]{5,4,3,2,1,0:T(8,128)S(1)}, f32[1,1,1,8,8,128]{5,4,3,2,1,0:T(8,128)}, u32[]{:S(2)}) copy-start(f32[1,1,1,8,8,128]{5,4,3,2,1,0:T(8,128)} %get-tuple-element.24) | copy-start | bytes 98308
  68.4 4.8 %copy-start.18 = (f32[1,1,1,8,8,128]{5,4,3,2,1,0:T(8,128)S(1)}, f32[1,1,1,8,8,128]{5,4,3,2,1,0:T(8,128)}, u32[]{:S(2)}) copy-start(f32[1,1,1,8,8,128]{5,4,3,2,1,0:T(8,128)} %get-tuple-element.25) | copy-start | bytes 98308
  68.4 4.8 %copy-start.19 = (f32[1,1,1,8,8,128]{5,4,3,2,1,0:T(8,128)S(1)}, f32[1,1,1,8,8,128]{5,4,3,2,1,0:T(8,128)}, u32[]{:S(2)}) copy-start(f32[1,1,1,8,8,128]{5,4,3,2,1,0:T(8,128)} %get-tuple-element.26) | copy-start | bytes 98308
  68.4 4.8 %copy-start.20 = (f32[1,1,1,8,8,128]{5,4,3,2,1,0:T(8,128)S(1)}, f32[1,1,1,8,8,128]{5,4,3,2,1,0:T(8,128)}, u32[]{:S(2)}) copy-start(f32[1,1,1,8,8,128]{5,4,3,2,1,0:T(8,128)} %get-tuple-element.27) | copy-start | bytes 98308
  69.4 3.8 %copy-start.43 = (f32[1,1,1,8,8,128]{5,4,3,2,1,0:T(8,128)S(1)}, f32[1,1,1,8,8,128]{5,4,3,2,1,0:T(8,128)}, u32[]{:S(2)}) copy-start(f32[1,1,1,8,8,128]{5,4,3,2,1,0:T(8,128)} %get-tuple-element.160) | copy-start | bytes 98308
  69.4 3.9 %copy-start.44 = (f32[1,1,1,8,8,128]{5,4,3,2,1,0:T(8,128)S(1)}, f32[1,1,1,8,8,128]{5,4,3,2,1,0:T(8,128)}, u32[]{:S(2)}) copy-start(f32[1,1,1,8,8,128]{5,4,3,2,1,0:T(8,128)} %get-tuple-element.161) | copy-start | bytes 98308
  69.4 3.9 %copy-start.45 = (f32[1,1,1,8,8,128]{5,4,3,2,1,0:T(8,128)S(1)}, f32[1,1,1,8,8,128]{5,4,3,2,1,0:T(8,128)}, u32[]{:S(2)}) copy-start(f32[1,1,1,8,8,128]{5,4,3,2,1,0:T(8,128)} %get-tuple-element.182) | copy-start | bytes 98308
  69.4 3.9 %copy-start.46 = (f32[1,1,1,8,8,128]{5,4,3,2,1,0:T(8,128)S(1)}, f32[1,1,1,8,8,128]{5,4,3,2,1,0:T(8,128)}, u32[]{:S(2)}) copy-start(f32[1,1,1,8,8,128]{5,4,3,2,1,0:T(8,128)} %get-tuple-element.183) | copy-start | bytes 98308
  69.4 3.9 %copy-start.47 = (f32[1,1,1,8,8,128]{5,4,3,2,1,0:T(8,128)S(1)}, f32[1,1,1,8,8,128]{5,4,3,2,1,0:T(8,128)}, u32[]{:S(2)}) copy-start(f32[1,1,1,8,8,128]{5,4,3,2,1,0:T(8,128)} %get-tuple-element.184) | copy-start | bytes 98308
  69.4 3.9 %copy-start.48 = (f32[1,1,1,8,8,128]{5,4,3,2,1,0:T(8,128)S(1)}, f32[1,1,1,8,8,128]{5,4,3,2,1,0:T(8,128)}, u32[]{:S(2)}) copy-start(f32[1,1,1,8,8,128]{5,4,3,2,1,0:T(8,128)} %get-tuple-element.163) | copy-start | bytes 98308
  77.9 4.5 %copy-start.31 = (f32[1,1,1,8,8,128]{5,4,3,2,1,0:T(8,128)S(1)}, f32[1,1,1,8,8,128]{5,4,3,2,1,0:T(8,128)}, u32[]{:S(2)}) copy-start(f32[1,1,1,8,8,128]{5,4,3,2,1,0:T(8,128)} %get-tuple-element.194) | copy-start | bytes 98308
  77.9 4.5 %copy-start.32 = (f32[1,1,1,8,8,128]{5,4,3,2,1,0:T(8,128)S(1)}, f32[1,1,1,8,8,128]{5,4,3,2,1,0:T(8,128)}, u32[]{:S(2)}) copy-start(f32[1,1,1,8,8,128]{5,4,3,2,1,0:T(8,128)} %get-tuple-element.195) | copy-start | bytes 98308
  77.9 4.5 %copy-start.33 = (f32[1,1,1,8,8,128]{5,4,3,2,1,0:T(8,128)S(1)}, f32[1,1,1,8,8,128]{5,4,3,2,1,0:T(8,128)}, u32[]{:S(2)}) copy-start(f32[1,1,1,8,8,128]{5,4,3,2,1,0:T(8,128)} %get-tuple-element.196) | copy-start | bytes 98308
  77.9 4.5 %copy-start.37 = (f32[1,1,1,8,8,128]{5,4,3,2,1,0:T(8,128)S(1)}, f32[1,1,1,8,8,128]{5,4,3,2,1,0:T(8,128)}, u32[]{:S(2)}) copy-start(f32[1,1,1,8,8,128]{5,4,3,2,1,0:T(8,128)} %get-tuple-element.165) | copy-start | bytes 98308
  77.9 4.5 %copy-start.38 = (f32[1,1,1,8,8,128]{5,4,3,2,1,0:T(8,128)S(1)}, f32[1,1,1,8,8,128]{5,4,3,2,1,0:T(8,128)}, u32[]{:S(2)}) copy-start(f32[1,1,1,8,8,128]{5,4,3,2,1,0:T(8,128)} %get-tuple-element.166) | copy-start | bytes 98308
  77.9 4.5 %copy-start.39 = (f32[1,1,1,8,8,128]{5,4,3,2,1,0:T(8,128)S(1)}, f32[1,1,1,8,8,128]{5,4,3,2,1,0:T(8,128)}, u32[]{:S(2)}) copy-start(f32[1,1,1,8,8,128]{5,4,3,2,1,0:T(8,128)} %get-tuple-element.167) | copy-start | bytes 98308
  77.9 4.5 %copy-start.49 = (f32[1,1,1,8,8,128]{5,4,3,2,1,0:T(8,128)S(1)}, f32[1,1,1,8,8,128]{5,4,3,2,1,0:T(8,128)}, u32[]{:S(2)}) copy-start(f32[1,1,1,8,8,128]{5,4,3,2,1,0:T(8,128)} %get-tuple-element.110) | copy-start | bytes 98308
  77.9 4.5 %copy-start.50 = (f32[1,1,1,8,8,128]{5,4,3,2,1,0:T(8,128)S(1)}, f32[1,1,1,8,8,128]{5,4,3,2,1,0:T(8,128)}, u32[]{:S(2)}) copy-start(f32[1,1,1,8,8,128]{5,4,3,2,1,0:T(8,128)} %get-tuple-element.111) | copy-start | bytes 98308
  78.0 4.5 %copy-start.51 = (f32[1,1,1,8,8,128]{5,4,3,2,1,0:T(8,128)S(1)}, f32[1,1,1,8,8,128]{5,4,3,2,1,0:T(8,128)}, u32[]{:S(2)}) copy-start(f32[1,1,1,8,8,128]{5,4,3,2,1,0:T(8,128)} %get-tuple-element.112) | copy-start | bytes 98308
  78.8 3.7 %copy-start.52 = (f32[1,1,1,8,8,128]{5,4,3,2,1,0:T(8,128)S(1)}, f32[1,1,1,8,8,128]{5,4,3,2,1,0:T(8,128)}, u32[]{:S(2)}) copy-start(f32[1,1,1,8,8,128]{5,4,3,2,1,0:T(8,128)} %get-tuple-element.113) | copy-start | bytes 98308
  78.8 3.7 %copy-start.53 = (f32[1,1,1,8,8,128]{5,4,3,2,1,0:T(8,128)S(1)}, f32[1,1,1,8,8,128]{5,4,3,2,1,0:T(8,128)}, u32[]{:S(2)}) copy-start(f32[1,1,1,8,8,128]{5,4,3,2,1,0:T(8,128)} %get-tuple-element.114) | copy-start | bytes 98308
  78.8 3.7 %copy-start.54 = (f32[1,1,1,8,8,128]{5,4,3,2,1,0:T(8,128)S(1)}, f32[1,1,1,8,8,128]{5,4,3,2,1,0:T(8,128)}, u32[]{:S(2)}) copy-start(f32[1,1,1,8,8,128]{5,4,3,2,1,0:T(8,128)} %get-tuple-element.115) | copy-start | bytes 98308
  85.5 11.4 %copy-start.60 = (s32[1,64,1]{1,2,0:T(1,128)S(1)}, s32[1,64,1]{1,2,0:T(1,128)}, u32[]{:S(2)}) copy-start(s32[1,64,1]{1,2,0:T(1,128)} %broadcast_bitcast_fusion) | copy-start | bytes 772
  85.5 22.7 %copy-start.56 = (f32[63,64]{0,1:T(8,128)S(1)}, f32[63,64]{0,1:T(8,128)}, u32[]{:S(2)}) copy-start(f32[63,64]{0,1:T(8,128)} %constant.25.clone.1) | copy-start | bytes 48388
  86.8 10.1 %collective-permute-start.6 = (f32[2,8,128]{2,1,0:T(8,128)S(1)}, f32[2,8,128]{2,1,0:T(8,128)S(1)}, u32[]{:S(2)}, u32[]{:S(2)}) collective-permute-start(f32[2,8,128]{2,1,0:T(8,128)S(1)} %get-tuple-element.212), channel_id=1, source_target_pairs={{0,16},{16,32},{32,48},{48,64},{64,80},{80,96},{96,112},{112,128},... | collective-permute-start | bytes 24584 | tf_op jit(solution)/shard_map/ppermute | solution.py:22
  94.9 8.9 %collective-permute-start.7 = (f32[2,8,128]{2,1,0:T(8,128)S(1)}, f32[2,8,128]{2,1,0:T(8,128)S(1)}, u32[]{:S(2)}, u32[]{:S(2)}) collective-permute-start(f32[2,8,128]{2,1,0:T(8,128)S(1)} %get-tuple-element.213), channel_id=1, source_target_pairs={{16,0},{32,16},{48,32},{64,48},{80,64},{96,80},{112,96},{128,112},... | collective-permute-start | bytes 24584 | tf_op jit(solution)/shard_map/ppermute | solution.py:24
  103.8 4.6 %collective-permute-start.8 = (f32[12,2,128]{2,1,0:T(2,128)S(1)}, f32[12,2,128]{2,1,0:T(2,128)S(1)}, u32[]{:S(2)}, u32[]{:S(2)}) collective-permute-start(f32[12,2,128]{2,1,0:T(2,128)S(1)} %get-tuple-element.203), channel_id=1, source_target_pairs={{0,1},{1,2},{2,3},{3,4},{4,5},{5,6},{6,7},{7,8},{8,9},{9,10},{10,1... | collective-permute-start | bytes 36872 | tf_op jit(solution)/shard_map/ppermute | solution.py:22
  106.9 7.1 %collective-permute-start.9 = (f32[12,2,128]{2,1,0:T(2,128)S(1)}, f32[12,2,128]{2,1,0:T(2,128)S(1)}, u32[]{:S(2)}, u32[]{:S(2)}) collective-permute-start(f32[12,2,128]{2,1,0:T(2,128)S(1)} %get-tuple-element.204), channel_id=1, source_target_pairs={{1,0},{2,1},{3,2},{4,3},{5,4},{6,5},{7,6},{8,7},{9,8},{10,9},{11,1... | collective-permute-start | bytes 36872 | tf_op jit(solution)/shard_map/ppermute | solution.py:24
  108.4 6.5 %copy-start.57 = (f32[8,8,128]{2,1,0:T(8,128)S(1)}, f32[8,8,128]{2,1,0:T(8,128)}, u32[]{:S(2)}) copy-start(f32[8,8,128]{2,1,0:T(8,128)} %get-tuple-element.207) | copy-start | bytes 98308
  108.4 6.5 %copy-start.58 = (f32[8,8,128]{2,1,0:T(8,128)S(1)}, f32[8,8,128]{2,1,0:T(8,128)}, u32[]{:S(2)}) copy-start(f32[8,8,128]{2,1,0:T(8,128)} %get-tuple-element.208) | copy-start | bytes 98308
  114.3 114.4 %copy-start.59 = (f32[64]{0:T(128)S(1)}, f32[64]{0:T(128)}, u32[]{:S(2)}) copy-start(f32[64]{0:T(128)} %param.15) | copy-start | bytes 772
  114.8 118.4 %copy-start.30 = (f32[8,8,128]{2,1,0:T(8,128)}, f32[8,8,128]{2,1,0:T(8,128)S(1)}, u32[]{:S(2)}) copy-start(f32[8,8,128]{2,1,0:T(8,128)S(1)} %get-tuple-element.6) | copy-start | bytes 98308
  (23 other events, 45.6 us)
where the time goes:
time: 236 us; the launch traced here: 234 us
  blocking collectives  112 us (47%)
  local copies, waits for them, and re-layouts  46.5 us (20%)
  starting transfers between devices  32.5 us (14%)
  waiting for transfers between devices  20.3 us (9%)
  matrix products  11.7 us (5%)
  other arithmetic  9.3 us (4%)
    psum x1, blocking collectives, bisect_round(): volumes = lax.psum(partial_volumes, ('gx', 'gy'))  112 us
    another operation x8, local copies, waits for them, and re-layouts, element_terms(): vectors.append(jnp.stack(row_list))  31 us
    ppermute x4, starting transfers between devices, with_halo(): lax.ppermute(tail, axis, [(i, (i + 1) % count) for i in range(ends)])  15.6 us
    ppermute x4, waiting for transfers between devices, with_halo(): lax.ppermute(head, axis, [((i + 1) % count, i) for i in range(ends)])  15.3 us
    ppermute x4, starting transfers between devices, with_halo(): lax.ppermute(head, axis, [((i + 1) % count, i) for i in range(ends)])  13.3 us
    slice x9, local copies, waits for them, and re-layouts, element_terms(): extended[pair_index, member, component, corner_x:corner_x + cells_x, corn...  8.41 us
    dot_general x4, matrix products, element_terms(): jnp.dot(mass_matrix, adjoint_rows, precision=lax.Precision.HIGHEST)  7.02 us
    ppermute x2, waiting for transfers between devices, from_behind(): lax.ppermute(value, axis, [(source, source + steps) for source in range(i...  4.95 us
  transfers between devices with their start and end apart: 10, of which 4 were waited for; matrix products, arithmetic and copies ran while one was open for 3% of the time, Pallas kernels for 0%

commit v1 on v0

--- a/solution.py
+++ b/solution.py
@@ -173,7 +173,7 @@
         partial_volumes = (
             jnp.sum(fields_of, axis=(1, 2)).reshape(len(midpoints), REGIONS, band_cells).sum(axis=2)
         )
-        volumes = lax.psum(partial_volumes, ("gx", "gy"))
+        volumes = lax.psum(lax.psum(partial_volumes, "gx"), "gy")
         position = jnp.zeros((REGIONS,), jnp.int32)
         for depth in range(levels):
             middle = jnp.sqrt(low_end * high_end)

time: 236 us -> 379 us (1.61)
  the two profiles are of different devices: /device:TPU:1 before, /device:TPU:256 now
where the time goes in v1:
time: 379 us; the launch traced here: 377 us
  blocking collectives  253 us (67%)
  local copies, waits for them, and re-layouts  46.4 us (12%)
  starting transfers between devices  38.7 us (10%)
  waiting for transfers between devices  16.2 us (4%)
  matrix products  11.6 us (3%)
  other arithmetic  9.26 us (2%)
    psum x2, blocking collectives, bisect_round(): volumes = lax.psum(lax.psum(partial_volumes, 'gx'), 'gy')  253 us
    another operation x8, local copies, waits for them, and re-layouts, element_terms(): vectors.append(jnp.stack(row_list))  30.8 us
    ppermute x4, starting transfers between devices, with_halo(): lax.ppermute(head, axis, [((i + 1) % count, i) for i in range(ends)])  18.5 us
    ppermute x4, waiting for transfers between devices, with_halo(): lax.ppermute(head, axis, [((i + 1) % count, i) for i in range(ends)])  12.2 us
    ppermute x2, starting transfers between devices, from_behind(): lax.ppermute(value, axis, [(source, source + steps) for source in range(i...  11 us
    ppermute x4, starting transfers between devices, with_halo(): lax.ppermute(tail, axis, [(i, (i + 1) % count) for i in range(ends)])  9.22 us
    slice x9, local copies, waits for them, and re-layouts, element_terms(): extended[pair_index, member, component, corner_x:corner_x + cells_x, corn...  8.3 us
  transfers between devices with their start and end apart: 10, of which 4 were waited for; matrix products, arithmetic and copies ran while one was open for 2% of the time, Pallas kernels for 0%

profile of v1, /device:TPU:256, one launch (start us, length us, event | category | flops | bytes accessed | tf_op | source)
XLA Modules:
  0.0 376.7 jit_solution(18373509777490403360)
XLA Ops:
  1.4 6.3 %collective-permute-start.1 = (f32[2,8,128]{2,1,0:T(8,128)S(1)}, f32[2,8,128]{2,1,0:T(8,128)S(1)}, u32[]{:S(2)}, u32[]{:S(2)}) collective-permute-start(f32[2,8,128]{2,1,0:T(8,128)S(1)} %get-tuple-element.214), channel_id=1, source_target_pairs={{16,0},{32,16},{48,32},{64,48},{80,64},{96,80},{112,96},{128,112},... | collective-permute-start | bytes 24584 | tf_op jit(solution)/shard_map/ppermute | solution.py:24
  7.7 1.9 collective-permute-start
  10.4 1.2 broadcast_multiply_fusion
  11.6 9.7 %collective-permute-start.4 = (f32[4,2,3,1,8,128]{5,4,3,2,1,0:T(8,128)S(1)}, f32[4,2,3,1,8,128]{5,4,3,2,1,0:T(8,128)S(1)}, u32[]{:S(2)}, u32[]{:S(2)}) collective-permute-start(f32[4,2,3,1,8,128]{5,4,3,2,1,0:T(8,128)S(1)} %slice.2424), channel_id=1, source_target_pairs={{16,0},{32,16},{48,32},{64,48},{80,64},{96,80},{112,96},{128,112},... | collective-permute-start | bytes 294920 | tf_op jit(solution)/shard_map/ppermute | solution.py:34
  23.0 2.6 collective-permute-start.2
  25.6 1.3 collective-permute-start.3
  27.5 4.0 %collective-permute-done.3 = f32[12,2,128]{2,1,0:T(2,128)S(1)} collective-permute-done((f32[12,2,128]{2,1,0:T(2,128)S(1)}, f32[12,2,128]{2,1,0:T(2,128)S(1)}, u32[]{:S(2)}, u32[]{:S(2)}) %collective-permute-start.3) | collective-permute-done | bytes 12320 | tf_op jit(solution)/shard_map/ppermute | solution.py:24
  31.7 1.3 collective-permute-start.5
  35.3 4.0 %collective-permute-done.5 = f32[4,2,3,9,1,128]{5,3,4,2,1,0:T(8,128)S(1)} collective-permute-done((f32[4,2,3,9,1,128]{5,3,4,2,1,0:T(8,128)S(1)}, f32[4,2,3,9,1,128]{5,3,4,2,1,0:T(8,128)S(1)}, u32[]{:S(2)}, u32[]{:S(2)}) %collective-permute-start.5) | collective-permute-done | bytes 110624 | tf_op jit(solution)/shard_map/ppermute | solution.py:34
  40.4 1.0 pad_slice_fusion.79
  41.4 1.1 pad_slice_fusion.48
  42.4 0.9 fusion.372
  43.3 1.1 fusion.373
  44.4 0.9 fusion.374
  45.3 3.7 stack.24
  49.0 5.8 %stack.25 = f32[24,8192]{1,0:T(8,128)} concatenate(f32[1,8192]{1,0:T(1,128)} %bitcast.571, f32[1,8192]{1,0:T(1,128)} %bitcast.570, f32[1,8192]{1,0:T(1,128)} %bitcast.588, f32[1,8192]{1,0:T(1,128)} %bitcast.468, f32[1,8192]{1,0:T(1,128)} %bitcast.469, f32[1,8192]{1,0:T(1,128)} %bitcast.470, f32[1,8192]{1,0:T(1,128)} %bitcast.617, f32[1,8192]{1,0:T(1,128)} %bitcast.616, ...), dimensions={0} | concatenate | bytes 1572864 | tf_op jit(solution)/shard_map/stack | solution.py:90
  54.8 2.7 fusion.17
  57.4 1.5 fusion.13
  58.9 3.7 stack.31
  62.6 5.8 %stack.30 = f32[24,8192]{1,0:T(8,128)} concatenate(f32[1,8192]{1,0:T(1,128)} %bitcast.558, f32[1,8192]{1,0:T(1,128)} %bitcast.557, f32[1,8192]{1,0:T(1,128)} %bitcast.556, f32[1,8192]{1,0:T(1,128)} %bitcast.466, f32[1,8192]{1,0:T(1,128)} %bitcast.479, f32[1,8192]{1,0:T(1,128)} %bitcast.480, f32[1,8192]{1,0:T(1,128)} %bitcast.513, f32[1,8192]{1,0:T(1,128)} %bitcast.512, ...), dimensions={0} | concatenate | bytes 1572864 | tf_op jit(solution)/shard_map/stack | solution.py:90
  68.4 2.7 fusion.20
  71.0 1.5 fusion.16
  72.5 0.9 fusion.375
  73.5 0.9 pad_slice_fusion.49
  74.5 3.6 stack.27
  78.4 3.6 stack.26
  82.1 0.9 fusion.18
  83.1 0.8 fusion.14
  84.1 3.4 stack.29
  87.6 1.2 stack.28
  88.8 0.9 fusion.19
  89.7 0.9 fusion.15
  90.6 1.2 fusion.98
  91.9 1.9 collective-permute-start.6
  93.8 9.7 %collective-permute-start.7 = (f32[2,8,128]{2,1,0:T(8,128)S(1)}, f32[2,8,128]{2,1,0:T(8,128)S(1)}, u32[]{:S(2)}, u32[]{:S(2)}) collective-permute-start(f32[2,8,128]{2,1,0:T(8,128)S(1)} %get-tuple-element.213), channel_id=1, source_target_pairs={{16,0},{32,16},{48,32},{64,48},{80,64},{96,80},{112,96},{128,112},... | collective-permute-start | bytes 24584 | tf_op jit(solution)/shard_map/ppermute | solution.py:24
  103.5 1.3 collective-permute-done.7
  104.8 2.8 collective-permute-start.8
  107.6 1.3 collective-permute-start.9
  109.1 6.9 %collective-permute-done.9 = f32[12,2,128]{2,1,0:T(2,128)S(1)} collective-permute-done((f32[12,2,128]{2,1,0:T(2,128)S(1)}, f32[12,2,128]{2,1,0:T(2,128)S(1)}, u32[]{:S(2)}, u32[]{:S(2)}) %collective-permute-start.9) | collective-permute-done | bytes 12320 | tf_op jit(solution)/shard_map/ppermute | solution.py:24
  116.8 0.9 fusion.12
  118.0 173.5 %psum.14 = f32[63,64]{1,0:T(8,128)S(1)} all-reduce(f32[63,64]{1,0:T(8,128)S(1)} %copy.118), channel_id=1, replica_groups=mesh['gx'=32,'gy'=16] {'gx'}, use_global_device_ids=true, to_apply=%region_10.11 | all-reduce | flops 4032 | bytes 32256 | tf_op jit(solution)/shard_map/psum | solution.py:176
  291.5 79.2 %psum.15 = f32[63,64]{1,0:T(8,128)S(1)} all-reduce(f32[63,64]{1,0:T(8,128)S(1)} %psum.14), channel_id=1, replica_groups=mesh['gx'=32,'gy'=16] {'gy'}, use_global_device_ids=true, to_apply=%region_11.12 | all-reduce | flops 4032 | bytes 32256 | tf_op jit(solution)/shard_map/psum | solution.py:176
  370.7 0.8 gather_fusion
  371.6 0.8 gather_fusion.1
  372.4 0.8 gather_fusion.2
  373.3 0.8 gather_fusion.3
  374.1 0.8 gather_fusion.4
  375.0 0.8 gather_fusion.5
  (183 shorter events, 9.9 us)
Async XLA Ops:
  0.6 54.1 %copy-start = (f32[24,24]{1,0:T(8,128)S(1)}, f32[24,24]{1,0:T(8,128)}, u32[]{:S(2)}) copy-start(f32[24,24]{1,0:T(8,128)} %param.14) | copy-start | bytes 6916
  0.6 21.7 %copy-start.3 = (f32[8,8,128]{2,1,0:T(8,128)S(1)}, f32[8,8,128]{2,1,0:T(8,128)}, u32[]{:S(2)}) copy-start(f32[8,8,128]{2,1,0:T(8,128)} %param.9) | copy-start | bytes 98308
  1.4 21.5 %collective-permute-start.1 = (f32[2,8,128]{2,1,0:T(8,128)S(1)}, f32[2,8,128]{2,1,0:T(8,128)S(1)}, u32[]{:S(2)}, u32[]{:S(2)}) collective-permute-start(f32[2,8,128]{2,1,0:T(8,128)S(1)} %get-tuple-element.214), channel_id=1, source_target_pairs={{16,0},{32,16},{48,32},{64,48},{80,64},{96,80},{112,96},{128,112},... | collective-permute-start | bytes 24584 | tf_op jit(solution)/shard_map/ppermute | solution.py:24
  7.7 14.6 %collective-permute-start = (f32[2,8,128]{2,1,0:T(8,128)S(1)}, f32[2,8,128]{2,1,0:T(8,128)S(1)}, u32[]{:S(2)}, u32[]{:S(2)}) collective-permute-start(f32[2,8,128]{2,1,0:T(8,128)S(1)} %get-tuple-element.215), channel_id=1, source_target_pairs={{0,16},{16,32},{32,48},{48,64},{64,80},{80,96},{96,112},{112,128},... | collective-permute-start | bytes 24584 | tf_op jit(solution)/shard_map/ppermute | solution.py:22
  11.6 20.0 %collective-permute-start.4 = (f32[4,2,3,1,8,128]{5,4,3,2,1,0:T(8,128)S(1)}, f32[4,2,3,1,8,128]{5,4,3,2,1,0:T(8,128)S(1)}, u32[]{:S(2)}, u32[]{:S(2)}) collective-permute-start(f32[4,2,3,1,8,128]{5,4,3,2,1,0:T(8,128)S(1)} %slice.2424), channel_id=1, source_target_pairs={{16,0},{32,16},{48,32},{64,48},{80,64},{96,80},{112,96},{128,112},... | collective-permute-start | bytes 294920 | tf_op jit(solution)/shard_map/ppermute | solution.py:34
  23.0 4.5 %collective-permute-start.2 = (f32[12,2,128]{2,1,0:T(2,128)S(1)}, f32[12,2,128]{2,1,0:T(2,128)S(1)}, u32[]{:S(2)}, u32[]{:S(2)}) collective-permute-start(f32[12,2,128]{2,1,0:T(2,128)S(1)} %get-tuple-element.205), channel_id=1, source_target_pairs={{0,1},{1,2},{2,3},{3,4},{4,5},{5,6},{6,7},{7,8},{8,9},{9,10},{10,1... | collective-permute-start | bytes 36872 | tf_op jit(solution)/shard_map/ppermute | solution.py:22
  25.6 5.9 %collective-permute-start.3 = (f32[12,2,128]{2,1,0:T(2,128)S(1)}, f32[12,2,128]{2,1,0:T(2,128)S(1)}, u32[]{:S(2)}, u32[]{:S(2)}) collective-permute-start(f32[12,2,128]{2,1,0:T(2,128)S(1)} %get-tuple-element.206), channel_id=1, source_target_pairs={{1,0},{2,1},{3,2},{4,3},{5,4},{6,5},{7,6},{8,7},{9,8},{10,9},{11,1... | collective-permute-start | bytes 36872 | tf_op jit(solution)/shard_map/ppermute | solution.py:24
  31.7 7.6 %collective-permute-start.5 = (f32[4,2,3,9,1,128]{5,3,4,2,1,0:T(8,128)S(1)}, f32[4,2,3,9,1,128]{5,3,4,2,1,0:T(8,128)S(1)}, u32[]{:S(2)}, u32[]{:S(2)}) collective-permute-start(f32[4,2,3,9,1,128]{5,3,4,2,1,0:T(8,128)S(1)} %copy.114), channel_id=1, source_target_pairs={{1,0},{2,1},{3,2},{4,3},{5,4},{6,5},{7,6},{8,7},{9,8},{10,9},{11,1... | collective-permute-start | bytes 331784 | tf_op jit(solution)/shard_map/ppermute | solution.py:34
  49.0 8.4 %copy-start.4 = (f32[24,24]{1,0:T(8,128)S(1)}, f32[24,24]{1,0:T(8,128)}, u32[]{:S(2)}) copy-start(f32[24,24]{1,0:T(8,128)} %param.13) | copy-start | bytes 6916
  73.4 4.8 %copy-start.10 = (f32[1,1,1,8,8,128]{5,4,3,2,1,0:T(8,128)S(1)}, f32[1,1,1,8,8,128]{5,4,3,2,1,0:T(8,128)}, u32[]{:S(2)}) copy-start(f32[1,1,1,8,8,128]{5,4,3,2,1,0:T(8,128)} %get-tuple-element.17) | copy-start | bytes 98308
  73.4 4.8 %copy-start.11 = (f32[1,1,1,8,8,128]{5,4,3,2,1,0:T(8,128)S(1)}, f32[1,1,1,8,8,128]{5,4,3,2,1,0:T(8,128)}, u32[]{:S(2)}) copy-start(f32[1,1,1,8,8,128]{5,4,3,2,1,0:T(8,128)} %get-tuple-element.18) | copy-start | bytes 98308
  73.4 4.8 %copy-start.12 = (f32[1,1,1,8,8,128]{5,4,3,2,1,0:T(8,128)S(1)}, f32[1,1,1,8,8,128]{5,4,3,2,1,0:T(8,128)}, u32[]{:S(2)}) copy-start(f32[1,1,1,8,8,128]{5,4,3,2,1,0:T(8,128)} %get-tuple-element.19) | copy-start | bytes 98308
  73.4 4.8 %copy-start.13 = (f32[1,1,1,8,8,128]{5,4,3,2,1,0:T(8,128)S(1)}, f32[1,1,1,8,8,128]{5,4,3,2,1,0:T(8,128)}, u32[]{:S(2)}) copy-start(f32[1,1,1,8,8,128]{5,4,3,2,1,0:T(8,128)} %get-tuple-element.20) | copy-start | bytes 98308
  73.4 4.8 %copy-start.14 = (f32[1,1,1,8,8,128]{5,4,3,2,1,0:T(8,128)S(1)}, f32[1,1,1,8,8,128]{5,4,3,2,1,0:T(8,128)}, u32[]{:S(2)}) copy-start(f32[1,1,1,8,8,128]{5,4,3,2,1,0:T(8,128)} %get-tuple-element.21) | copy-start | bytes 98308
  73.5 4.8 %copy-start.15 = (f32[1,1,1,8,8,128]{5,4,3,2,1,0:T(8,128)S(1)}, f32[1,1,1,8,8,128]{5,4,3,2,1,0:T(8,128)}, u32[]{:S(2)}) copy-start(f32[1,1,1,8,8,128]{5,4,3,2,1,0:T(8,128)} %get-tuple-element.22) | copy-start | bytes 98308
  73.5 4.8 %copy-start.16 = (f32[1,1,1,8,8,128]{5,4,3,2,1,0:T(8,128)S(1)}, f32[1,1,1,8,8,128]{5,4,3,2,1,0:T(8,128)}, u32[]{:S(2)}) copy-start(f32[1,1,1,8,8,128]{5,4,3,2,1,0:T(8,128)} %get-tuple-element.23) | copy-start | bytes 98308
  73.5 4.8 %copy-start.17 = (f32[1,1,1,8,8,128]{5,4,3,2,1,0:T(8,128)S(1)}, f32[1,1,1,8,8,128]{5,4,3,2,1,0:T(8,128)}, u32[]{:S(2)}) copy-start(f32[1,1,1,8,8,128]{5,4,3,2,1,0:T(8,128)} %get-tuple-element.24) | copy-start | bytes 98308
  73.5 4.8 %copy-start.18 = (f32[1,1,1,8,8,128]{5,4,3,2,1,0:T(8,128)S(1)}, f32[1,1,1,8,8,128]{5,4,3,2,1,0:T(8,128)}, u32[]{:S(2)}) copy-start(f32[1,1,1,8,8,128]{5,4,3,2,1,0:T(8,128)} %get-tuple-element.25) | copy-start | bytes 98308
  73.5 4.8 %copy-start.19 = (f32[1,1,1,8,8,128]{5,4,3,2,1,0:T(8,128)S(1)}, f32[1,1,1,8,8,128]{5,4,3,2,1,0:T(8,128)}, u32[]{:S(2)}) copy-start(f32[1,1,1,8,8,128]{5,4,3,2,1,0:T(8,128)} %get-tuple-element.26) | copy-start | bytes 98308
  73.5 4.8 %copy-start.20 = (f32[1,1,1,8,8,128]{5,4,3,2,1,0:T(8,128)S(1)}, f32[1,1,1,8,8,128]{5,4,3,2,1,0:T(8,128)}, u32[]{:S(2)}) copy-start(f32[1,1,1,8,8,128]{5,4,3,2,1,0:T(8,128)} %get-tuple-element.27) | copy-start | bytes 98308
  74.5 3.8 %copy-start.43 = (f32[1,1,1,8,8,128]{5,4,3,2,1,0:T(8,128)S(1)}, f32[1,1,1,8,8,128]{5,4,3,2,1,0:T(8,128)}, u32[]{:S(2)}) copy-start(f32[1,1,1,8,8,128]{5,4,3,2,1,0:T(8,128)} %get-tuple-element.160) | copy-start | bytes 98308
  74.5 3.9 %copy-start.44 = (f32[1,1,1,8,8,128]{5,4,3,2,1,0:T(8,128)S(1)}, f32[1,1,1,8,8,128]{5,4,3,2,1,0:T(8,128)}, u32[]{:S(2)}) copy-start(f32[1,1,1,8,8,128]{5,4,3,2,1,0:T(8,128)} %get-tuple-element.161) | copy-start | bytes 98308
  74.5 3.9 %copy-start.45 = (f32[1,1,1,8,8,128]{5,4,3,2,1,0:T(8,128)S(1)}, f32[1,1,1,8,8,128]{5,4,3,2,1,0:T(8,128)}, u32[]{:S(2)}) copy-start(f32[1,1,1,8,8,128]{5,4,3,2,1,0:T(8,128)} %get-tuple-element.182) | copy-start | bytes 98308
  74.5 3.9 %copy-start.46 = (f32[1,1,1,8,8,128]{5,4,3,2,1,0:T(8,128)S(1)}, f32[1,1,1,8,8,128]{5,4,3,2,1,0:T(8,128)}, u32[]{:S(2)}) copy-start(f32[1,1,1,8,8,128]{5,4,3,2,1,0:T(8,128)} %get-tuple-element.183) | copy-start | bytes 98308
  74.5 3.9 %copy-start.47 = (f32[1,1,1,8,8,128]{5,4,3,2,1,0:T(8,128)S(1)}, f32[1,1,1,8,8,128]{5,4,3,2,1,0:T(8,128)}, u32[]{:S(2)}) copy-start(f32[1,1,1,8,8,128]{5,4,3,2,1,0:T(8,128)} %get-tuple-element.184) | copy-start | bytes 98308
  74.5 3.9 %copy-start.48 = (f32[1,1,1,8,8,128]{5,4,3,2,1,0:T(8,128)S(1)}, f32[1,1,1,8,8,128]{5,4,3,2,1,0:T(8,128)}, u32[]{:S(2)}) copy-start(f32[1,1,1,8,8,128]{5,4,3,2,1,0:T(8,128)} %get-tuple-element.163) | copy-start | bytes 98308
  83.0 4.5 %copy-start.31 = (f32[1,1,1,8,8,128]{5,4,3,2,1,0:T(8,128)S(1)}, f32[1,1,1,8,8,128]{5,4,3,2,1,0:T(8,128)}, u32[]{:S(2)}) copy-start(f32[1,1,1,8,8,128]{5,4,3,2,1,0:T(8,128)} %get-tuple-element.194) | copy-start | bytes 98308
  83.0 4.5 %copy-start.32 = (f32[1,1,1,8,8,128]{5,4,3,2,1,0:T(8,128)S(1)}, f32[1,1,1,8,8,128]{5,4,3,2,1,0:T(8,128)}, u32[]{:S(2)}) copy-start(f32[1,1,1,8,8,128]{5,4,3,2,1,0:T(8,128)} %get-tuple-element.195) | copy-start | bytes 98308
  83.0 4.5 %copy-start.33 = (f32[1,1,1,8,8,128]{5,4,3,2,1,0:T(8,128)S(1)}, f32[1,1,1,8,8,128]{5,4,3,2,1,0:T(8,128)}, u32[]{:S(2)}) copy-start(f32[1,1,1,8,8,128]{5,4,3,2,1,0:T(8,128)} %get-tuple-element.196) | copy-start | bytes 98308
  83.0 4.5 %copy-start.37 = (f32[1,1,1,8,8,128]{5,4,3,2,1,0:T(8,128)S(1)}, f32[1,1,1,8,8,128]{5,4,3,2,1,0:T(8,128)}, u32[]{:S(2)}) copy-start(f32[1,1,1,8,8,128]{5,4,3,2,1,0:T(8,128)} %get-tuple-element.165) | copy-start | bytes 98308
  83.0 4.5 %copy-start.38 = (f32[1,1,1,8,8,128]{5,4,3,2,1,0:T(8,128)S(1)}, f32[1,1,1,8,8,128]{5,4,3,2,1,0:T(8,128)}, u32[]{:S(2)}) copy-start(f32[1,1,1,8,8,128]{5,4,3,2,1,0:T(8,128)} %get-tuple-element.166) | copy-start | bytes 98308
  83.0 4.5 %copy-start.39 = (f32[1,1,1,8,8,128]{5,4,3,2,1,0:T(8,128)S(1)}, f32[1,1,1,8,8,128]{5,4,3,2,1,0:T(8,128)}, u32[]{:S(2)}) copy-start(f32[1,1,1,8,8,128]{5,4,3,2,1,0:T(8,128)} %get-tuple-element.167) | copy-start | bytes 98308
  83.0 4.5 %copy-start.49 = (f32[1,1,1,8,8,128]{5,4,3,2,1,0:T(8,128)S(1)}, f32[1,1,1,8,8,128]{5,4,3,2,1,0:T(8,128)}, u32[]{:S(2)}) copy-start(f32[1,1,1,8,8,128]{5,4,3,2,1,0:T(8,128)} %get-tuple-element.110) | copy-start | bytes 98308
  83.0 4.5 %copy-start.50 = (f32[1,1,1,8,8,128]{5,4,3,2,1,0:T(8,128)S(1)}, f32[1,1,1,8,8,128]{5,4,3,2,1,0:T(8,128)}, u32[]{:S(2)}) copy-start(f32[1,1,1,8,8,128]{5,4,3,2,1,0:T(8,128)} %get-tuple-element.111) | copy-start | bytes 98308
  83.0 4.5 %copy-start.51 = (f32[1,1,1,8,8,128]{5,4,3,2,1,0:T(8,128)S(1)}, f32[1,1,1,8,8,128]{5,4,3,2,1,0:T(8,128)}, u32[]{:S(2)}) copy-start(f32[1,1,1,8,8,128]{5,4,3,2,1,0:T(8,128)} %get-tuple-element.112) | copy-start | bytes 98308
  83.9 3.7 copy-start.52
  83.9 3.7 copy-start.53
  83.9 3.7 copy-start.54
  90.6 12.9 %copy-start.60 = (s32[1,64,1]{1,2,0:T(1,128)S(1)}, s32[1,64,1]{1,2,0:T(1,128)}, u32[]{:S(2)}) copy-start(s32[1,64,1]{1,2,0:T(1,128)} %broadcast_bitcast_fusion) | copy-start | bytes 772
  90.6 18.3 %copy-start.56 = (f32[63,64]{0,1:T(8,128)S(1)}, f32[63,64]{0,1:T(8,128)}, u32[]{:S(2)}) copy-start(f32[63,64]{0,1:T(8,128)} %constant.25.clone.1) | copy-start | bytes 48388
  91.9 11.6 %collective-permute-start.6 = (f32[2,8,128]{2,1,0:T(8,128)S(1)}, f32[2,8,128]{2,1,0:T(8,128)S(1)}, u32[]{:S(2)}, u32[]{:S(2)}) collective-permute-start(f32[2,8,128]{2,1,0:T(8,128)S(1)} %get-tuple-element.212), channel_id=1, source_target_pairs={{0,16},{16,32},{32,48},{48,64},{64,80},{80,96},{96,112},{112,128},... | collective-permute-start | bytes 24584 | tf_op jit(solution)/shard_map/ppermute | solution.py:22
  93.8 11.0 %collective-permute-start.7 = (f32[2,8,128]{2,1,0:T(8,128)S(1)}, f32[2,8,128]{2,1,0:T(8,128)S(1)}, u32[]{:S(2)}, u32[]{:S(2)}) collective-permute-start(f32[2,8,128]{2,1,0:T(8,128)S(1)} %get-tuple-element.213), channel_id=1, source_target_pairs={{16,0},{32,16},{48,32},{64,48},{80,64},{96,80},{112,96},{128,112},... | collective-permute-start | bytes 24584 | tf_op jit(solution)/shard_map/ppermute | solution.py:24
  104.8 4.3 %collective-permute-start.8 = (f32[12,2,128]{2,1,0:T(2,128)S(1)}, f32[12,2,128]{2,1,0:T(2,128)S(1)}, u32[]{:S(2)}, u32[]{:S(2)}) collective-permute-start(f32[12,2,128]{2,1,0:T(2,128)S(1)} %get-tuple-element.203), channel_id=1, source_target_pairs={{0,1},{1,2},{2,3},{3,4},{4,5},{5,6},{6,7},{7,8},{8,9},{9,10},{10,1... | collective-permute-start | bytes 36872 | tf_op jit(solution)/shard_map/ppermute | solution.py:22
  107.6 8.4 %collective-permute-start.9 = (f32[12,2,128]{2,1,0:T(2,128)S(1)}, f32[12,2,128]{2,1,0:T(2,128)S(1)}, u32[]{:S(2)}, u32[]{:S(2)}) collective-permute-start(f32[12,2,128]{2,1,0:T(2,128)S(1)} %get-tuple-element.204), channel_id=1, source_target_pairs={{1,0},{2,1},{3,2},{4,3},{5,4},{6,5},{7,6},{8,7},{9,8},{10,9},{11,1... | collective-permute-start | bytes 36872 | tf_op jit(solution)/shard_map/ppermute | solution.py:24
  109.1 7.7 %copy-start.57 = (f32[8,8,128]{2,1,0:T(8,128)S(1)}, f32[8,8,128]{2,1,0:T(8,128)}, u32[]{:S(2)}) copy-start(f32[8,8,128]{2,1,0:T(8,128)} %get-tuple-element.207) | copy-start | bytes 98308
  109.1 7.7 %copy-start.58 = (f32[8,8,128]{2,1,0:T(8,128)S(1)}, f32[8,8,128]{2,1,0:T(8,128)}, u32[]{:S(2)}) copy-start(f32[8,8,128]{2,1,0:T(8,128)} %get-tuple-element.208) | copy-start | bytes 98308
  116.2 255.3 %copy-start.59 = (f32[64]{0:T(128)S(1)}, f32[64]{0:T(128)}, u32[]{:S(2)}) copy-start(f32[64]{0:T(128)} %param.15) | copy-start | bytes 772
  116.8 259.3 %copy-start.30 = (f32[8,8,128]{2,1,0:T(8,128)}, f32[8,8,128]{2,1,0:T(8,128)S(1)}, u32[]{:S(2)}) copy-start(f32[8,8,128]{2,1,0:T(8,128)S(1)} %get-tuple-element.6) | copy-start | bytes 98308
  (23 other events, 45.7 us)
